TPU v7x, 512 devices: a whole 4x4x16 slice. The times are simulated.
512 devices in a mesh: kv: 8 (over y, core), pages: 64 (over x, z).
Axes of the slice: x: 4, y: 4, z: 16, core: 2. Of those that a mesh axis runs over, the one named last changes fastest.
Arguments:
- tokens: int32 [2, 64], replicated, may hold values from 0 to 31999
- prompt_len: int32 [8], replicated, may hold values from 193 to 8192, as said below
- page_table: int32 [8, 64], replicated, may hold values from -1 to 511, as said below
- parents: int32 [2, 64], replicated, may hold values from 0 to 63, as said below
- embedding: bfloat16 [32000, 7168], P('kv', 'pages'), may hold values from -6 to 6
- norm_gain: bfloat16 [7168], P('pages'), may hold values from 0.099609375 to 1.8984375
- w_qkv: bfloat16 [7168, 9216], P('pages', 'kv'), may hold values from -0.0625 to 0.0625
- w_out: bfloat16 [7168, 7168], P('kv', 'pages'), may hold values from -0.8984375 to 0.8984375
- history: bfloat16 [2, 64, 13, 1024], P(None, None, None, 'kv'), may hold values from -6 to 6
- kv_pool: bfloat16 [2, 512, 128, 1024], P(None, 'pages', None, 'kv'), may hold values from -400 to 400
Outputs:
- hidden: bfloat16 [2, 64, 7168], P(None, None, 'pages')
- history_out: bfloat16 [2, 64, 15, 1024], P(None, None, None, 'kv')
Inputs may be any that keep to these rules, and one draw needn't show every extreme that they name: `prompt_len`: each prompt is either long, within 512 tokens below 8192, or short, within 64 tokens below 256; some group's prompt has exactly 8192 tokens. For j below prompt_len[g] / 128 rounded up, page_table[g, j] is the slot holding tokens j * 128 to j * 128 + 127 of group g's prompt; no slot is named twice; all other entries are -1. parents[t, b] is a beam of b's group; at the first step the first and the last beam of every group continue their own history.
All inputs are finite; a program needn't handle non-finite values.
Results may differ from a plain program's by a relative error of at most 0.015.
The roundings to bfloat16 on the way count: a program that leaves them out, or rounds other values in their place, can miss the bound.
Values may be sent and summed in bfloat16 or wider, within the bound.
No kernel may reach another device: no remote copies, remote signals or barrier semaphores. Data moves between devices by JAX's collectives and lax.ppermute only.
A program may use at most 128 MiB of HBM per device.

v0:
```python
import jax
import jax.numpy as jnp
from jax import lax
from jax.sharding import PartitionSpec as P

D = 7168
KV_HEADS = 8
HEAD_DIM = 128
GROUPS = 8
BEAMS = 8
PRIOR = 13
PAGE = 128
PER_KV = 7
HISTORY = 15
MAX_PAGES = 64
THETA = 5000000.0
EPSILON = 1e-05
NEGATIVE = -1e30


def merged(part, axis, combine):
    gathered = jax.tree.map(lambda a: lax.all_gather(a, axis), part)

    def take(source):
        return jax.tree.map(lambda a: lax.dynamic_index_in_dim(a, source, 0, False), gathered)

    return lax.fori_loop(
        1, lax.axis_size(axis), lambda source, state: combine(state, take(source)), take(0)
    )


def rotate(values, positions):
    half_dim = HEAD_DIM // 2
    frequency = THETA ** (-(2.0 * jnp.arange(half_dim, dtype=jnp.float32)) / HEAD_DIM)
    angles = positions.astype(jnp.float32)[:, None] * frequency[None, :]
    cosine = jnp.cos(angles)[:, None, None, :]
    sine_part = jnp.sin(angles)[:, None, None, :]
    lower_part = values[..., :half_dim]
    upper_part = values[..., half_dim:]
    return jnp.concatenate(
        [
            lower_part * cosine - upper_part * sine_part,
            upper_part * cosine + lower_part * sine_part,
        ],
        axis=-1,
    )


def finish_rows(summed, norm_sums, row_ids, prompt_len, num_seqs, local_heads):
    inverse_rms = lax.rsqrt(norm_sums / D + EPSILON)
    projected = (summed * inverse_rms[:, None]).reshape(-1, local_heads, PER_KV + 2, HEAD_DIM)
    positions = jnp.take(prompt_len, row_ids % num_seqs // BEAMS) + PRIOR + row_ids // num_seqs
    turned = rotate(projected[:, :, : PER_KV + 1], positions)
    return jnp.concatenate([turned, projected[:, :, PER_KV + 1 :]], axis=2).astype(jnp.bfloat16)


def combine(earlier, later):
    peak = jnp.maximum(earlier[0], later[0])
    weight_one = jnp.exp(earlier[0] - peak)
    weight_two = jnp.exp(later[0] - peak)
    return (
        peak,
        earlier[1] * weight_one + later[1] * weight_two,
        earlier[2] * weight_one[:, None] + later[2] * weight_two[:, None],
    )


def per_device(
    tokens, prompt_len, page_table, parents, embedding, norm_gain, w_qkv, w_out, history, kv_pool
):
    num_steps, num_seqs = tokens.shape
    row_count = num_steps * num_seqs
    local_heads = KV_HEADS // lax.axis_size("kv")
    kv_width = local_heads * HEAD_DIM
    inv_root = 1.0 / jnp.sqrt(jnp.float32(HEAD_DIM))
    vocab_local = embedding.shape[0]
    local_ids = tokens.reshape(-1) - lax.axis_index("kv") * vocab_local
    inside = (local_ids >= 0) & (local_ids < vocab_local)
    picked = jnp.take(embedding, jnp.clip(local_ids, 0, vocab_local - 1), axis=0)
    found = jnp.where(inside[:, None], picked.astype(jnp.float32), 0.0)
    embedded = lax.psum(found.astype(jnp.bfloat16), "kv")
    widened = embedded.astype(jnp.float32)
    squares = jnp.sum(widened * widened, axis=1)
    normed = (widened * norm_gain.astype(jnp.float32)).astype(jnp.bfloat16)
    partial_value = jnp.dot(normed, w_qkv, preferred_element_type=jnp.float32)
    summed, norm_sums = lax.psum((partial_value, squares), "pages")
    projected = finish_rows(
        summed, norm_sums, jnp.arange(row_count, dtype=jnp.int32), prompt_len, num_seqs, local_heads
    )
    queries = projected[:, :, :PER_KV]
    fresh_kv = jnp.stack([projected[:, :, PER_KV], projected[:, :, PER_KV + 1]]).reshape(
        2, num_steps, num_seqs, kv_width
    )
    buffer = jnp.concatenate(
        [history, jnp.zeros((2, num_seqs, num_steps, kv_width), jnp.bfloat16)], axis=2
    )
    snapshots = []
    for step_index in range(num_steps):
        buffer = jnp.take(buffer, parents[step_index], axis=1)
        buffer = buffer.at[:, :, PRIOR + step_index].set(fresh_kv[:, step_index])
        snapshots.append(buffer)
    stacked = jnp.stack(snapshots)
    tail_keys = stacked[:, 0].reshape(num_steps, num_seqs, HISTORY, local_heads, HEAD_DIM)
    tail_vals = stacked[:, 1].reshape(num_steps, num_seqs, HISTORY, local_heads, HEAD_DIM)
    step_query = queries.reshape(num_steps, num_seqs, local_heads, PER_KV, HEAD_DIM)
    tail_len = PRIOR + 1 + jnp.arange(num_steps, dtype=jnp.int32)
    tail_valid = (jnp.arange(HISTORY, dtype=jnp.int32)[None, :] < tail_len[:, None])[
        :, None, None, None, :
    ]
    tail_scores = (
        jnp.einsum("tbkhd,tblkd->tbkhl", step_query, tail_keys, preferred_element_type=jnp.float32)
        * inv_root
    )
    tail_scores = jnp.where(tail_valid, tail_scores, NEGATIVE)
    tail_peak = jnp.max(tail_scores, axis=-1)
    tail_exp = jnp.where(tail_valid, jnp.exp(tail_scores - tail_peak[..., None]), 0.0)
    tail_total = jnp.sum(tail_exp, axis=-1)
    tail_acc = jnp.einsum(
        "tbkhl,tblkd->tbkhd",
        tail_exp.astype(jnp.bfloat16),
        tail_vals,
        preferred_element_type=jnp.float32,
    )
    tail_part = (tail_peak.reshape(-1), tail_total.reshape(-1), tail_acc.reshape(-1, HEAD_DIM))
    slot_rows = kv_pool.shape[1]
    slot_ids = lax.axis_index("pages") * slot_rows + jnp.arange(slot_rows, dtype=jnp.int32)
    matches = page_table[:, :, None] == slot_ids[None, None, :]
    slot_used = jnp.any(matches, axis=(0, 1))
    owner_group = jnp.sum(
        jnp.where(matches, jnp.arange(GROUPS, dtype=jnp.int32)[:, None, None], 0), axis=(0, 1)
    )
    page_number = jnp.sum(
        jnp.where(matches, jnp.arange(MAX_PAGES, dtype=jnp.int32)[None, :, None], 0), axis=(0, 1)
    )
    length = jnp.take(prompt_len, owner_group)
    live_tok = slot_used[:, None] & (
        page_number[:, None] * PAGE + jnp.arange(PAGE, dtype=jnp.int32)[None, :] < length[:, None]
    )
    live_full = live_tok[None, :, None, :]
    grouped = queries.reshape(num_steps, GROUPS, BEAMS, local_heads, PER_KV, HEAD_DIM)
    chosen = jnp.take(grouped, owner_group, axis=1)
    query_rows = num_steps * BEAMS * PER_KV
    chosen = jnp.transpose(chosen, (3, 1, 0, 2, 4, 5)).reshape(
        local_heads, slot_rows, query_rows, HEAD_DIM
    )
    page_keys = jnp.transpose(
        kv_pool[0].reshape(slot_rows, PAGE, local_heads, HEAD_DIM), (2, 0, 1, 3)
    )
    page_vals = jnp.transpose(
        kv_pool[1].reshape(slot_rows, PAGE, local_heads, HEAD_DIM), (2, 0, 1, 3)
    )
    scores = (
        jnp.einsum("ksqd,kspd->ksqp", chosen, page_keys, preferred_element_type=jnp.float32)
        * inv_root
    )
    scores = jnp.where(live_full, scores, NEGATIVE)
    slot_peak = jnp.max(scores, axis=-1)
    slot_exp = jnp.where(live_full, jnp.exp(scores - slot_peak[..., None]), 0.0)
    slot_total = jnp.sum(slot_exp, axis=-1)
    slot_acc = jnp.einsum(
        "ksqp,kspd->ksqd",
        slot_exp.astype(jnp.bfloat16),
        page_vals,
        preferred_element_type=jnp.float32,
    )
    member = (owner_group[:, None] == jnp.arange(GROUPS, dtype=jnp.int32)[None, :]) & slot_used[
        :, None
    ]
    spread = jnp.where(member[None, :, :, None], slot_peak[:, :, None, :], NEGATIVE)
    group_peak = jnp.max(spread, axis=1)
    slot_base = jnp.take(group_peak, owner_group, axis=1)
    weight = jnp.where(slot_used[None, :, None], jnp.exp(slot_peak - slot_base), 0.0)
    member_f = member.astype(jnp.float32)
    group_total = jnp.einsum(
        "sg,ksq->kgq", member_f, slot_total * weight, precision=lax.Precision.HIGHEST
    )
    group_acc = jnp.einsum(
        "sg,ksqd->kgqd", member_f, slot_acc * weight[..., None], precision=lax.Precision.HIGHEST
    )
    order_small = (2, 1, 3, 0, 4)
    peak_rows = jnp.transpose(
        group_peak.reshape(local_heads, GROUPS, num_steps, BEAMS, PER_KV), order_small
    )
    total_rows = jnp.transpose(
        group_total.reshape(local_heads, GROUPS, num_steps, BEAMS, PER_KV), order_small
    )
    acc_rows = jnp.transpose(
        group_acc.reshape(local_heads, GROUPS, num_steps, BEAMS, PER_KV, HEAD_DIM),
        (2, 1, 3, 0, 4, 5),
    )
    local_part = (peak_rows.reshape(-1), total_rows.reshape(-1), acc_rows.reshape(-1, HEAD_DIM))
    joined = merged(local_part, "pages", combine)
    complete = combine(joined, tail_part)
    attended = (complete[2] / complete[1][:, None]).astype(jnp.bfloat16)
    flat_heads = attended.reshape(row_count, local_heads * PER_KV * HEAD_DIM)
    head_terms = jnp.dot(flat_heads, w_out, preferred_element_type=jnp.float32)
    mixed_out = lax.psum(head_terms.astype(jnp.bfloat16), "kv").astype(jnp.float32) + widened
    return (mixed_out.astype(jnp.bfloat16).reshape(num_steps, num_seqs, -1), buffer)


def solution(mesh):
    placed = (
        P(),
        P(),
        P(),
        P(),
        P("kv", "pages"),
        P("pages"),
        P("pages", "kv"),
        P("kv", "pages"),
        P(None, None, None, "kv"),
        P(None, "pages", None, "kv"),
    )
    return jax.shard_map(
        per_device,
        mesh=mesh,
        in_specs=placed,
        out_specs=(P(None, None, "pages"), P(None, None, None, "kv")),
        check_vma=False,
    )
```

profile of v0, /device:TPU:2, one launch (start us, length us, event | category | flops | bytes accessed | tf_op | source)
XLA Modules:
  0.0 760.0 jit_solution(2022923756878189014)
XLA Ops:
  9.6 1.9 copy.93
  12.4 25.9 %psum.28 = bf16[128,112]{0,1:T(8,128)(2,1)S(1)} all-reduce(bf16[128,112]{0,1:T(8,128)(2,1)S(1)} %select_convert_fusion), channel_id=1, replica_groups=mesh['kv'=8,'pages'=64] {'kv'}, use_global_device_ids=true, to_apply=%region_3.4 | all-reduce | flops 14336 | bytes 57344 | tf_op jit(solution)/shard_map/psum | solution.py:81
  41.4 1.6 fusion.63
  44.3 128.2 %psum.30 = f32[128]{0:T(128)S(1)} all-reduce(f32[128]{0:T(128)S(1)} %fusion.34), channel_id=1, replica_groups=mesh['kv'=8,'pages'=64] {'pages'}, use_global_device_ids=true, to_apply=%region_6.7 | all-reduce | flops 128 | bytes 1024 | tf_op jit(solution)/shard_map/psum | solution.py:86
  172.6 5.0 fusion.54
  177.9 131.7 %all-reduce.3.cloned.1.call-done = f32[128,1152]{1,0:T(8,128)} async-done(((f32[128,1152]{1,0:T(8,128)}), f32[128,1152]{1,0:T(8,128)}) %all-reduce.3.cloned.1.call-update) | async-done | bytes 589840 | tf_op jit(solution)/shard_map/psum | solution.py:86
  317.3 1.4 copy.106
  319.9 1.6 gather_fusion.4
  323.3 80.6 %all-gather = f32[64,1,896]{2,1,0:T(1,128)S(1)} all-gather(f32[1,1,896]{2,1,0:T(1,128)S(1)} %reshape.757), channel_id=1, replica_groups=mesh['kv'=8,'pages'=64] {'pages'}, dimensions={0}, use_global_device_ids=true | all-gather | bytes 232960 | tf_op jit(solution)/shard_map/all_gather | solution.py:22
  404.6 82.0 %all-gather.1 = f32[64,1,896]{2,1,0:T(1,128)S(1)} all-gather(f32[1,1,896]{2,1,0:T(1,128)S(1)} %reshape.759), channel_id=1, replica_groups=mesh['kv'=8,'pages'=64] {'pages'}, dimensions={0}, use_global_device_ids=true | all-gather | bytes 232960 | tf_op jit(solution)/shard_map/all_gather | solution.py:22
  489.3 1.6 gather_fusion.5
  493.7 88.1 %all-gather.4.cloned.1.call-done = f32[64,896,128]{2,1,0:T(8,128)} async-done(((f32[1,896,128]{2,1,0:T(8,128)}), f32[64,896,128]{2,1,0:T(8,128)}) %all-gather.4.cloned.1.call-update) | async-done | bytes 29360144 | tf_op jit(solution)/shard_map/all_gather | solution.py:22
  582.9 142.8 %while.21 = (s32[]{:T(128)}, f32[896]{0:T(1024)S(1)}, f32[896]{0:T(1024)S(1)}, f32[896,128]{1,0:T(8,128)S(1)}, f32[64,896]{1,0:T(8,128)}, /*index=5*/f32[64,896]...) while((s32[]{:T(128)}, f32[896]{0:T(1024)S(1)}, f32[896]{0:T(1024)S(1)}, ...), condition=%wide.region_11.12_spmd, body=%wide.region_10.11_spmd.sunk | while | flops 349445 | bytes 1426575 | solution.py:27
  583.7 1.4 fusion.71
  586.0 1.4 fusion.71
  588.2 1.4 fusion.71
  590.5 1.4 fusion.71
  592.8 1.4 fusion.71
  595.0 1.4 fusion.71
  597.3 1.4 fusion.71
  599.6 1.4 fusion.71
  601.8 1.4 fusion.71
  604.1 1.4 fusion.71
  606.4 1.4 fusion.71
  608.6 1.4 fusion.71
  615.4 1.4 fusion.71
  617.7 1.4 fusion.71
  624.5 1.4 fusion.71
  626.8 1.4 fusion.71
  635.8 1.4 fusion.71
  638.1 1.4 fusion.71
  647.2 1.4 fusion.71
  649.4 1.4 fusion.71
  658.5 1.4 fusion.71
  660.8 1.4 fusion.71
  667.6 1.4 fusion.71
  669.8 1.4 fusion.71
  678.9 1.4 fusion.71
  681.2 1.4 fusion.71
  690.2 1.4 fusion.71
  692.5 1.4 fusion.71
  701.6 1.4 fusion.71
  703.8 1.4 fusion.71
  710.6 1.4 fusion.71
  712.9 1.4 fusion.71
  722.0 1.4 fusion.71
  724.2 1.4 fusion.71
  727.5 24.9 %psum.31 = bf16[128,112]{0,1:T(8,128)(2,1)S(1)} all-reduce(bf16[128,112]{0,1:T(8,128)(2,1)S(1)} %convolution_convert_fusion), channel_id=1, replica_groups=mesh['kv'=8,'pages'=64] {'kv'}, use_global_device_ids=true, to_apply=%region_14.16 | all-reduce | flops 14336 | bytes 57344 | tf_op jit(solution)/shard_map/psum | solution.py:197
  (247 shorter events, 120.3 us)
Async XLA Ops:
  7.2 31.1 %copy-start = (bf16[112,1152]{1,0:T(8,128)(2,1)S(1)}, bf16[112,1152]{1,0:T(8,128)(2,1)}, u32[]{:S(2)}) copy-start(bf16[112,1152]{1,0:T(8,128)(2,1)} %param.24) | copy-start | bytes 774148
  7.2 302.5 %all-reduce.3.cloned.1.call-start = ((), (), s32[]{:S(2)}) async-start(), calls=%async_computation | async-start | bytes 1179648 | tf_op jit(solution)/shard_map/psum | solution.py:86
  39.5 542.4 %all-gather.4.cloned.1.call-start = ((), (), s32[]{:S(2)}) async-start(), calls=%async_computation.1 | async-start | bytes 29818880 | tf_op jit(solution)/shard_map/all_gather | solution.py:22
Sparse Core Ops, SparseCore 0:
  39.6 270.0 all-reduce.2
  317.4 264.3 all-gather.3
where the time goes:
time: 768 us; the launch traced here: 760 us
  blocking collectives  342 us (45%)
  waiting for transfers between devices  220 us (29%)
  other arithmetic  104 us (14%)
  local copies, waits for them, and re-layouts  71.8 us (9%)
  between operations  14.5 us (2%)
    all_gather x2, blocking collectives, merged(): gathered = jax.tree.map(lambda a: lax.all_gather(a, axis), part)  163 us
    psum x1, waiting for transfers between devices, per_device(): summed, norm_sums = lax.psum((partial_value, squares), 'pages')  132 us
    psum x1, blocking collectives, per_device(): summed, norm_sums = lax.psum((partial_value, squares), 'pages')  128 us
    add x63, other arithmetic, combine(): earlier[2] * weight_one[:, None] + later[2] * weight_two[:, None]  89.9 us
    all_gather x1, waiting for transfers between devices, merged(): gathered = jax.tree.map(lambda a: lax.all_gather(a, axis), part)  88.1 us
    dynamic_slice x65, local copies, waits for them, and re-layouts, take(): lax.dynamic_index_in_dim(a, source, 0, False)  50.1 us
    psum x1, blocking collectives, per_device(): embedded = lax.psum(found.astype(jnp.bfloat16), 'kv')  25.9 us
    psum x1, blocking collectives, per_device(): lax.psum(head_terms.astype(jnp.bfloat16), 'kv').astype(jnp.float32)  24.9 us
  transfers between devices with their start and end apart: 2, of which 2 were waited for; matrix products, arithmetic and copies ran while one was open for 3% of the time, Pallas kernels for 0%

commit v1 on v0

--- a/solution.py
+++ b/solution.py
@@ -78,7 +78,7 @@
     inside = (local_ids >= 0) & (local_ids < vocab_local)
     picked = jnp.take(embedding, jnp.clip(local_ids, 0, vocab_local - 1), axis=0)
     found = jnp.where(inside[:, None], picked.astype(jnp.float32), 0.0)
-    embedded = lax.psum(found.astype(jnp.bfloat16), "kv")
+    embedded = jnp.sum(lax.all_gather(found.astype(jnp.bfloat16), "kv"), axis=0)
     widened = embedded.astype(jnp.float32)
     squares = jnp.sum(widened * widened, axis=1)
     normed = (widened * norm_gain.astype(jnp.float32)).astype(jnp.bfloat16)

time: 768 us -> 757 us (0.986)
  blocking collectives: 342 us -> 329 us
    psum x1 -> x0, blocking collectives: 25.9 us -> none  [per_device(): embedded = lax.psum(found.astype(jnp.bfloat16), 'kv')]
    all_gather x0 -> x1, blocking collectives: none -> 13.3 us  [per_device(): embedded = jnp.sum(lax.all_gather(found.astype(jnp.bfloat16), 'kv'), axis=0)]
where the time goes in v1:
time: 757 us; the launch traced here: 749 us
  blocking collectives  329 us (43%)
  waiting for transfers between devices  222 us (29%)
  other arithmetic  104 us (14%)
  local copies, waits for them, and re-layouts  71.8 us (9%)
  between operations  14.5 us (2%)
    all_gather x2, blocking collectives, merged(): gathered = jax.tree.map(lambda a: lax.all_gather(a, axis), part)  163 us
    psum x1, waiting for transfers between devices, per_device(): summed, norm_sums = lax.psum((partial_value, squares), 'pages')  134 us
    psum x1, blocking collectives, per_device(): summed, norm_sums = lax.psum((partial_value, squares), 'pages')  128 us
    add x63, other arithmetic, combine(): earlier[2] * weight_one[:, None] + later[2] * weight_two[:, None]  89.9 us
    all_gather x1, waiting for transfers between devices, merged(): gathered = jax.tree.map(lambda a: lax.all_gather(a, axis), part)  88.1 us
    dynamic_slice x65, local copies, waits for them, and re-layouts, take(): lax.dynamic_index_in_dim(a, source, 0, False)  50.1 us
    psum x1, blocking collectives, per_device(): lax.psum(head_terms.astype(jnp.bfloat16), 'kv').astype(jnp.float32)  24.9 us
  transfers between devices with their start and end apart: 2, of which 2 were waited for; matrix products, arithmetic and copies ran while one was open for 3% of the time, Pallas kernels for 0%

profile of v1, /device:TPU:2, one launch (start us, length us, event | category | flops | bytes accessed | tf_op | source)
XLA Modules:
  0.0 749.3 jit_solution(4908775873403111483)
XLA Ops:
  9.6 1.9 copy.118
  12.4 13.3 %all_gather.13 = bf16[8,128,112]{1,2,0:T(8,128)(2,1)S(1)} all-gather(bf16[1,128,112]{1,2,0:T(8,128)(2,1)S(1)} %select_convert_fusion), channel_id=1, replica_groups=mesh['kv'=8,'pages'=64] {'kv'}, dimensions={0}, use_global_device_ids=true | all-gather | bytes 258048 | tf_op jit(solution)/shard_map/all_gather | solution.py:81
  28.9 1.6 fusion.63
  31.8 128.1 %psum.22 = f32[128]{0:T(128)S(1)} all-reduce(f32[128]{0:T(128)S(1)} %fusion.34), channel_id=1, replica_groups=mesh['kv'=8,'pages'=64] {'pages'}, use_global_device_ids=true, to_apply=%region_6.7 | all-reduce | flops 128 | bytes 1024 | tf_op jit(solution)/shard_map/psum | solution.py:86
  160.0 5.0 fusion.54
  165.3 133.7 %all-reduce.3.cloned.1.call-done = f32[128,1152]{1,0:T(8,128)} async-done(((f32[128,1152]{1,0:T(8,128)}), f32[128,1152]{1,0:T(8,128)}) %all-reduce.3.cloned.1.call-update) | async-done | bytes 589840 | tf_op jit(solution)/shard_map/psum | solution.py:86
  306.6 1.4 copy.133
  309.2 1.6 gather_fusion.4
  312.7 80.7 %all-gather = f32[64,1,896]{2,1,0:T(1,128)S(1)} all-gather(f32[1,1,896]{2,1,0:T(1,128)S(1)} %reshape.808), channel_id=1, replica_groups=mesh['kv'=8,'pages'=64] {'pages'}, dimensions={0}, use_global_device_ids=true | all-gather | bytes 232960 | tf_op jit(solution)/shard_map/all_gather | solution.py:22
  394.1 81.9 %all-gather.1 = f32[64,1,896]{2,1,0:T(1,128)S(1)} all-gather(f32[1,1,896]{2,1,0:T(1,128)S(1)} %reshape.810), channel_id=1, replica_groups=mesh['kv'=8,'pages'=64] {'pages'}, dimensions={0}, use_global_device_ids=true | all-gather | bytes 232960 | tf_op jit(solution)/shard_map/all_gather | solution.py:22
  478.6 1.6 gather_fusion.5
  483.0 88.1 %all-gather.4.cloned.1.call-done = f32[64,896,128]{2,1,0:T(8,128)} async-done(((f32[1,896,128]{2,1,0:T(8,128)}), f32[64,896,128]{2,1,0:T(8,128)}) %all-gather.4.cloned.1.call-update) | async-done | bytes 29360144 | tf_op jit(solution)/shard_map/all_gather | solution.py:22
  572.2 142.8 %while.21 = (s32[]{:T(128)}, f32[896]{0:T(1024)S(1)}, f32[896]{0:T(1024)S(1)}, f32[896,128]{1,0:T(8,128)S(1)}, f32[64,896]{1,0:T(8,128)}, /*index=5*/f32[64,896]...) while((s32[]{:T(128)}, f32[896]{0:T(1024)S(1)}, f32[896]{0:T(1024)S(1)}, ...), condition=%wide.region_11.12_spmd, body=%wide.region_10.11_spmd.sunk | while | flops 349445 | bytes 1426575 | solution.py:27
  573.0 1.4 fusion.71
  575.3 1.4 fusion.71
  577.6 1.4 fusion.71
  579.8 1.4 fusion.71
  582.1 1.4 fusion.71
  584.4 1.4 fusion.71
  586.6 1.4 fusion.71
  588.9 1.4 fusion.71
  591.2 1.4 fusion.71
  593.4 1.4 fusion.71
  595.7 1.4 fusion.71
  598.0 1.4 fusion.71
  604.8 1.4 fusion.71
  607.0 1.4 fusion.71
  616.1 1.4 fusion.71
  618.4 1.4 fusion.71
  625.2 1.4 fusion.71
  627.4 1.4 fusion.71
  636.5 1.4 fusion.71
  638.8 1.4 fusion.71
  647.8 1.4 fusion.71
  650.1 1.4 fusion.71
  659.2 1.4 fusion.71
  661.4 1.4 fusion.71
  668.2 1.4 fusion.71
  670.5 1.4 fusion.71
  679.5 1.4 fusion.71
  681.8 1.4 fusion.71
  690.9 1.4 fusion.71
  693.1 1.4 fusion.71
  702.2 1.4 fusion.71
  704.5 1.4 fusion.71
  711.3 1.4 fusion.71
  713.5 1.4 fusion.71
  716.8 24.9 %psum.23 = bf16[128,112]{0,1:T(8,128)(2,1)S(1)} all-reduce(bf16[128,112]{0,1:T(8,128)(2,1)S(1)} %convolution_convert_fusion), channel_id=1, replica_groups=mesh['kv'=8,'pages'=64] {'kv'}, use_global_device_ids=true, to_apply=%region_14.16 | all-reduce | flops 14336 | bytes 57344 | tf_op jit(solution)/shard_map/psum | solution.py:197
  (248 shorter events, 120.4 us)
Async XLA Ops:
  7.2 18.6 %copy-start = (bf16[112,1152]{1,0:T(8,128)(2,1)S(1)}, bf16[112,1152]{1,0:T(8,128)(2,1)}, u32[]{:S(2)}) copy-start(bf16[112,1152]{1,0:T(8,128)(2,1)} %param.24) | copy-start | bytes 774148
  7.2 291.8 %all-reduce.3.cloned.1.call-start = ((), (), s32[]{:S(2)}) async-start(), calls=%async_computation | async-start | bytes 1179648 | tf_op jit(solution)/shard_map/psum | solution.py:86
  26.9 544.2 %all-gather.4.cloned.1.call-start = ((), (), s32[]{:S(2)}) async-start(), calls=%async_computation.1 | async-start | bytes 29818880 | tf_op jit(solution)/shard_map/all_gather | solution.py:22
Sparse Core Ops, SparseCore 0:
  27.1 271.9 all-reduce.2
  306.8 264.3 all-gather.3
